TPU v7x, 256 devices: a whole 4x4x8 slice. The times are simulated.
256 devices in a mesh: prow: 64 (over x, z, core), pcol: 4 (over y).
Axes of the slice: x: 4, y: 4, z: 8, core: 2. Of those that a mesh axis runs over, the one named last changes fastest.
Arguments:
- right_side: float32 [512, 65536], P('pcol', 'prow'), may hold values from -6 to 6
- factor: float32 [65536, 2048], P('prow', 'pcol'), may hold values from -0.125 to 0.125
- inverses: float32 [2048, 512], replicated, as said below
Outputs:
- solved: float32 [512, 65536], P('pcol', 'prow')
Inputs may be any that keep to these rules, and one draw needn't show every extreme that they name: Each 512 x 512 block of inverses is lower triangular with a positive diagonal.
All inputs are finite; a program needn't handle non-finite values.
Results may differ from a plain program's by a relative error of at most 0.0001.
Values sent between devices are 32-bit elements; how exact they have to be, the bound alone decides.
No kernel may reach another device: no remote copies, remote signals or barrier semaphores. Data moves between devices by JAX's collectives and lax.ppermute only.
A program may use at most 64 MiB of HBM per device.

v0:
```python
import jax
import jax.numpy as jnp
from jax import lax
from jax.sharding import PartitionSpec as P


def spread(block, axis, source):
    block = jnp.where(lax.axis_index(axis) == source, block, jnp.zeros_like(block))
    return lax.psum(block, axis)


def contract(left, right):
    return lax.dot_general(
        left,
        right,
        (((1,), (1,)), ((), ())),
        precision=lax.Precision.HIGHEST,
        preferred_element_type=jnp.float32,
    )


def per_device(right_side, factor, inverses):
    block = factor.shape[1]
    rhs_width = right_side.shape[0]
    sections = lax.axis_size("pcol")
    all_samples = rhs_width * sections
    row_at = lax.axis_index("prow")
    col_at = lax.axis_index("pcol")
    top_block = factor[:block]
    panel_own = jnp.zeros((all_samples, block), jnp.float32)
    solved_head = jnp.zeros((rhs_width, block), jnp.float32)
    own_panels = []
    for section in range(sections):
        current = right_side[:, :block]
        if section > 0:
            current = current - lax.psum_scatter(
                contract(panel_own, top_block), "pcol", scatter_dimension=0, tiled=True
            )
        block_inverse = inverses[section * block : (section + 1) * block]
        solved_part = contract(current, block_inverse)
        solved_head = jnp.where(row_at == section, solved_part, solved_head)
        gathered = lax.all_gather(solved_part, "pcol", axis=0, tiled=True)
        panel_full = spread(gathered, "prow", section)
        panel_own = jnp.where(col_at == section, panel_full, panel_own)
        own_panels.append(lax.dynamic_slice_in_dim(panel_full, col_at * rhs_width, rhs_width, 0))
    updated = right_side - lax.psum_scatter(
        contract(panel_own, factor), "pcol", scatter_dimension=0, tiled=True
    )
    head_block = jnp.where(row_at < sections, solved_head, updated[:, :block])
    return jnp.concatenate([head_block, updated[:, block:]], axis=1)


def solution(mesh):
    return jax.shard_map(
        per_device,
        mesh=mesh,
        in_specs=(P("pcol", "prow"), P("prow", "pcol"), P()),
        out_specs=P("pcol", "prow"),
        check_vma=False,
    )
```

profile of v0, /device:TPU:1, one launch (start us, length us, event | category | flops | bytes accessed | tf_op | source)
XLA Modules:
  0.0 1011.9 jit_solution(13477425533814743867)
XLA Ops:
  6.5 0.0 all-gather.5.cloned.1.call-start
  6.5 3.2 fusion.8
  9.7 0.0 copy-start
  9.7 0.0 all-gather.5.cloned.1.call-update
  9.7 0.0 all-reduce.5.cloned.1.call-start
  9.8 29.5 %all-gather.5.cloned.1.call-done = f32[512,512]{1,0:T(8,128)} async-done(((f32[128,512]{1,0:T(8,128)}), f32[512,512]{1,0:T(8,128)}) %all-gather.5.cloned.1.call-update) | async-done | bytes 1048592 | tf_op jit(solution)/shard_map/all_gather | solution.py:42
  39.3 1.1 broadcast_select_fusion.3
  40.4 0.0 all-reduce.5.cloned.1.call-update
  40.4 0.0 reduce-scatter.5.cloned.1.call-start
  40.5 0.0 copy-start.1
  40.5 187.1 %all-reduce.5.cloned.1.call-done = f32[512,512]{1,0:T(8,128)} async-done(((f32[512,512]{1,0:T(8,128)}), f32[512,512]{1,0:T(8,128)}) %all-reduce.5.cloned.1.call-update) | async-done | bytes 1048592 | tf_op jit(solution)/shard_map/psum | solution.py:9
  227.6 0.0 copy-done
  227.6 4.1 fusion.10
  231.7 0.0 reduce-scatter.5.cloned.1.call-update
  231.7 0.0 all-gather.7.cloned.1.call-start
  231.8 22.7 %reduce-scatter.5.cloned.1.call-done = f32[128,512]{1,0:T(8,128)} async-done(((f32[512,512]{1,0:T(8,128)}), f32[128,512]{1,0:T(8,128)}) %reduce-scatter.5.cloned.1.call-update) | async-done | bytes 262160 | tf_op jit(solution)/shard_map/reduce_scatter | solution.py:36
  254.5 0.0 copy-done.1
  254.5 3.2 fusion.6
  257.7 0.0 all-gather.7.cloned.1.call-update
  257.7 0.0 all-reduce.7.cloned.1.call-start
  257.8 26.9 %all-gather.7.cloned.1.call-done = f32[512,512]{1,0:T(8,128)} async-done(((f32[128,512]{1,0:T(8,128)}), f32[512,512]{1,0:T(8,128)}) %all-gather.7.cloned.1.call-update) | async-done | bytes 1048592 | tf_op jit(solution)/shard_map/all_gather | solution.py:42
  284.6 2.3 broadcast_select_fusion.2
  286.9 0.0 all-reduce.7.cloned.1.call-update
  286.9 0.0 reduce-scatter.7.cloned.1.call-start
  287.0 185.8 %all-reduce.7.cloned.1.call-done = f32[512,512]{1,0:T(8,128)} async-done(((f32[512,512]{1,0:T(8,128)}), f32[512,512]{1,0:T(8,128)}) %all-reduce.7.cloned.1.call-update) | async-done | bytes 1048592 | tf_op jit(solution)/shard_map/psum | solution.py:9
  472.8 1.4 select_select_fusion
  474.2 2.8 fusion.14
  477.1 0.0 reduce-scatter.7.cloned.1.call-update
  477.1 0.0 all-gather.9.cloned.1.call-start
  477.1 22.7 %reduce-scatter.7.cloned.1.call-done = f32[128,512]{1,0:T(8,128)} async-done(((f32[512,512]{1,0:T(8,128)}), f32[128,512]{1,0:T(8,128)}) %reduce-scatter.7.cloned.1.call-update) | async-done | bytes 262160 | tf_op jit(solution)/shard_map/reduce_scatter | solution.py:36
  499.9 3.3 fusion.4
  503.1 0.0 all-gather.9.cloned.1.call-update
  503.2 0.0 all-reduce.9.cloned.1.call-start
  503.2 26.9 %all-gather.9.cloned.1.call-done = f32[512,512]{1,0:T(8,128)} async-done(((f32[128,512]{1,0:T(8,128)}), f32[512,512]{1,0:T(8,128)}) %all-gather.9.cloned.1.call-update) | async-done | bytes 1048592 | tf_op jit(solution)/shard_map/all_gather | solution.py:42
  530.2 1.1 broadcast_select_fusion.1
  531.2 0.0 all-reduce.9.cloned.1.call-update
  531.3 0.0 reduce-scatter.9.cloned.1.call-start
  531.3 187.1 %all-reduce.9.cloned.1.call-done = f32[512,512]{1,0:T(8,128)} async-done(((f32[512,512]{1,0:T(8,128)}), f32[512,512]{1,0:T(8,128)}) %all-reduce.9.cloned.1.call-update) | async-done | bytes 1048592 | tf_op jit(solution)/shard_map/psum | solution.py:9
  718.4 2.8 fusion.12
  721.3 0.0 reduce-scatter.9.cloned.1.call-update
  721.3 0.0 all-gather.11.cloned.1.call-start
  721.4 25.3 %reduce-scatter.9.cloned.1.call-done = f32[128,512]{1,0:T(8,128)} async-done(((f32[512,512]{1,0:T(8,128)}), f32[128,512]{1,0:T(8,128)}) %reduce-scatter.9.cloned.1.call-update) | async-done | bytes 262160 | tf_op jit(solution)/shard_map/reduce_scatter | solution.py:36
  746.6 3.3 fusion.2
  749.9 0.0 all-gather.11.cloned.1.call-update
  749.9 0.0 all-reduce.11.cloned.1.call-start
  750.0 26.9 %all-gather.11.cloned.1.call-done = f32[512,512]{1,0:T(8,128)} async-done(((f32[128,512]{1,0:T(8,128)}), f32[512,512]{1,0:T(8,128)}) %all-gather.11.cloned.1.call-update) | async-done | bytes 1048592 | tf_op jit(solution)/shard_map/all_gather | solution.py:42
  776.8 1.1 broadcast_select_fusion
  777.9 0.0 all-reduce.11.cloned.1.call-update
  777.9 0.2 reduce-scatter.11.cloned.1.call-start
  778.2 186.9 %all-reduce.11.cloned.1.call-done = f32[512,512]{1,0:T(8,128)} async-done(((f32[512,512]{1,0:T(8,128)}), f32[512,512]{1,0:T(8,128)}) %all-reduce.11.cloned.1.call-update) | async-done | bytes 1048592 | tf_op jit(solution)/shard_map/psum | solution.py:9
  965.1 4.9 fusion
  970.0 0.0 copy-start.2
  970.0 0.0 copy-start.6
  970.0 0.0 reduce-scatter.11.cloned.1.call-update
  970.1 32.8 %reduce-scatter.11.cloned.1.call-done = f32[128,1024]{1,0:T(8,128)} async-done(((f32[512,1024]{1,0:T(8,128)}), f32[128,1024]{1,0:T(8,128)}) %reduce-scatter.11.cloned.1.call-update) | async-done | bytes 524304 | tf_op jit(solution)/shard_map/reduce_scatter | solution.py:46
  1002.9 0.0 copy-done.2
  1002.9 1.1 sub.15
  1004.0 0.0 copy-done.3
  1004.0 0.0 copy-done.4
  1004.0 0.0 copy-done.5
  1004.1 0.0 copy-done.6
  1004.1 0.2 slice_select_fusion
  1004.2 0.0 copy-start.7
  1004.2 0.8 copy-done.7
  (4 shorter events, 0.0 us)
Async XLA Ops:
  6.5 32.8 %all-gather.5.cloned.1.call-start = ((), (), s32[]{:S(2)}) async-start(), calls=%async_computation.4 | async-start | bytes 1310720 | tf_op jit(solution)/shard_map/all_gather | solution.py:42
  9.7 217.9 %copy-start = (f32[1024,512]{1,0:T(8,128)S(1)}, f32[1024,512]{1,0:T(8,128)}, u32[]{:S(2)}) copy-start(f32[1024,512]{1,0:T(8,128)} %param.4) | copy-start | bytes 6291460
  9.7 217.9 %all-reduce.5.cloned.1.call-start = ((), (), s32[]{:S(2)}) async-start(), calls=%async_computation.5 | async-start | bytes 2097152 | tf_op jit(solution)/shard_map/psum | solution.py:9
  40.4 214.1 %reduce-scatter.5.cloned.1.call-start = ((), (), s32[]{:S(2)}) async-start(), calls=%async_computation.6 | async-start | bytes 1310720 | tf_op jit(solution)/shard_map/reduce_scatter | solution.py:36
  40.5 214.0 %copy-start.1 = (f32[128,1024]{1,0:T(8,128)S(1)}, f32[128,1024]{1,0:T(8,128)}, u32[]{:S(2)}) copy-start(f32[128,1024]{1,0:T(8,128)} %param.3) | copy-start | bytes 1572868
  231.7 52.9 %all-gather.7.cloned.1.call-start = ((), (), s32[]{:S(2)}) async-start(), calls=%async_computation.7 | async-start | bytes 1310720 | tf_op jit(solution)/shard_map/all_gather | solution.py:42
  257.7 215.0 %all-reduce.7.cloned.1.call-start = ((), (), s32[]{:S(2)}) async-start(), calls=%async_computation.8 | async-start | bytes 2097152 | tf_op jit(solution)/shard_map/psum | solution.py:9
  286.9 212.9 %reduce-scatter.7.cloned.1.call-start = ((), (), s32[]{:S(2)}) async-start(), calls=%async_computation.9 | async-start | bytes 1310720 | tf_op jit(solution)/shard_map/reduce_scatter | solution.py:36
  477.1 53.1 %all-gather.9.cloned.1.call-start = ((), (), s32[]{:S(2)}) async-start(), calls=%async_computation.10 | async-start | bytes 1310720 | tf_op jit(solution)/shard_map/all_gather | solution.py:42
  503.2 215.3 %all-reduce.9.cloned.1.call-start = ((), (), s32[]{:S(2)}) async-start(), calls=%async_computation.11 | async-start | bytes 2097152 | tf_op jit(solution)/shard_map/psum | solution.py:9
  531.3 215.3 %reduce-scatter.9.cloned.1.call-start = ((), (), s32[]{:S(2)}) async-start(), calls=%async_computation.12 | async-start | bytes 1310720 | tf_op jit(solution)/shard_map/reduce_scatter | solution.py:36
  721.3 55.5 %all-gather.11.cloned.1.call-start = ((), (), s32[]{:S(2)}) async-start(), calls=%async_computation.13 | async-start | bytes 1310720 | tf_op jit(solution)/shard_map/all_gather | solution.py:42
  749.9 215.2 %all-reduce.11.cloned.1.call-start = ((), (), s32[]{:S(2)}) async-start(), calls=%async_computation.14 | async-start | bytes 2097152 | tf_op jit(solution)/shard_map/psum | solution.py:9
  777.9 225.0 %reduce-scatter.11.cloned.1.call-start = ((), (), s32[]{:S(2)}) async-start(), calls=%async_computation.15 | async-start | bytes 2621440 | tf_op jit(solution)/shard_map/reduce_scatter | solution.py:46
  970.0 32.9 %copy-start.2 = (f32[128,1024]{1,0:T(8,128)S(1)}, f32[128,1024]{1,0:T(8,128)}, u32[]{:S(2)}) copy-start(f32[128,1024]{1,0:T(8,128)} %param.3) | copy-start | bytes 1572868
  970.0 34.0 %copy-start.3 = (f32[128,512]{1,0:T(8,128)S(1)}, f32[128,512]{1,0:T(8,128)}, u32[]{:S(2)}) copy-start(f32[128,512]{1,0:T(8,128)} %fusion.6) | copy-start | bytes 786436
  970.0 34.0 %copy-start.4 = (f32[128,512]{1,0:T(8,128)S(1)}, f32[128,512]{1,0:T(8,128)}, u32[]{:S(2)}) copy-start(f32[128,512]{1,0:T(8,128)} %fusion.4) | copy-start | bytes 786436
  970.0 34.0 %copy-start.5 = (f32[128,512]{1,0:T(8,128)S(1)}, f32[128,512]{1,0:T(8,128)}, u32[]{:S(2)}) copy-start(f32[128,512]{1,0:T(8,128)} %fusion.2) | copy-start | bytes 786436
  970.0 34.0 %copy-start.6 = (f32[128,512]{1,0:T(8,128)S(1)}, f32[128,512]{1,0:T(8,128)}, u32[]{:S(2)}) copy-start(f32[128,512]{1,0:T(8,128)} %fusion.8) | copy-start | bytes 786436
  1004.2 0.8 copy-start.7
Sparse Core Ops, SparseCore 0:
  9.9 29.4 all-gather.4
  42.8 184.8 all-reduce.4
  231.8 22.6 reduce-scatter.4
  257.8 26.7 all-gather.6
  287.9 184.8 all-reduce.6
  477.2 22.6 reduce-scatter.6
  503.3 26.8 all-gather.8
  533.6 184.8 all-reduce.8
  721.4 25.1 reduce-scatter.8
  750.0 26.7 all-gather.10
  780.3 184.8 all-reduce.10
  970.2 32.6 reduce-scatter.10
where the time goes:
time: 1010 us
  waiting for transfers between devices  961 us (95%)
  matrix products  27.6 us (3%)
  between operations  13.7 us (1%)
    psum x4, waiting for transfers between devices, spread(): return lax.psum(block, axis)  747 us
    all_gather x4, waiting for transfers between devices, per_device(): gathered = lax.all_gather(solved_part, 'pcol', axis=0, tiled=True)  110 us
    reduce_scatter x3, waiting for transfers between devices, per_device(): lax.psum_scatter(contract(panel_own, top_block), 'pcol', scatter_dimensio...  70.7 us
    reduce_scatter x1, waiting for transfers between devices, per_device(): lax.psum_scatter(contract(panel_own, factor), 'pcol', scatter_dimension=0...  32.8 us
    dot_general x8, matrix products, contract(): lax.dot_general(left, right, (((1,), (1,)), ((), ())), precision=lax.Prec...  27.6 us
  transfers between devices with their start and end apart: 12, of which 12 were waited for; matrix products, arithmetic and copies ran while one was open for 0% of the time, Pallas kernels for 0%

commit v1 on v0

--- a/solution.py
+++ b/solution.py
@@ -39,7 +39,15 @@
         block_inverse = inverses[section * block : (section + 1) * block]
         solved_part = contract(current, block_inverse)
         solved_head = jnp.where(row_at == section, solved_part, solved_head)
-        gathered = lax.all_gather(solved_part, "pcol", axis=0, tiled=True)
+        gathered = jnp.concatenate(
+            lax.all_to_all(
+                jnp.stack([solved_part] * lax.axis_size("pcol"), 0),
+                axis_name="pcol",
+                split_axis=0,
+                concat_axis=0,
+            ),
+            axis=0,
+        )
         panel_full = spread(gathered, "prow", section)
         panel_own = jnp.where(col_at == section, panel_full, panel_own)
         own_panels.append(lax.dynamic_slice_in_dim(panel_full, col_at * rhs_width, rhs_width, 0))

time: 1010 us -> 970 us (0.960)
  waiting for transfers between devices: 961 us -> 900 us
  starting transfers between devices: 0.64 us -> 17.5 us
    all_gather x4 -> x0, waiting for transfers between devices: 110 us -> none  [per_device(): gathered = lax.all_gather(solved_part, 'pcol', axis=0, tiled=True)]
    all_to_all x0 -> x4, waiting for transfers between devices: none -> 52.6 us  [per_device(): lax.all_to_all(jnp.stack([solved_part] * lax.axis_size('pcol'), 0), axis_...]
    all_to_all x0 -> x4, starting transfers between devices: none -> 17 us  [per_device(): lax.all_to_all(jnp.stack([solved_part] * lax.axis_size('pcol'), 0), axis_...]
where the time goes in v1:
time: 970 us; the launch traced here: 969 us
  waiting for transfers between devices  900 us (93%)
  matrix products  24.7 us (3%)
  starting transfers between devices  17.5 us (2%)
  between operations  13.7 us (1%)
    psum x4, waiting for transfers between devices, spread(): return lax.psum(block, axis)  743 us
    reduce_scatter x3, waiting for transfers between devices, per_device(): lax.psum_scatter(contract(panel_own, top_block), 'pcol', scatter_dimensio...  70.8 us
    all_to_all x4, waiting for transfers between devices, per_device(): lax.all_to_all(jnp.stack([solved_part] * lax.axis_size('pcol'), 0), axis_...  52.6 us
    reduce_scatter x1, waiting for transfers between devices, per_device(): lax.psum_scatter(contract(panel_own, factor), 'pcol', scatter_dimension=0...  32.8 us
    dot_general x8, matrix products, contract(): lax.dot_general(left, right, (((1,), (1,)), ((), ())), precision=lax.Prec...  24.7 us
  transfers between devices with their start and end apart: 12, of which 12 were waited for; matrix products, arithmetic and copies ran while one was open for 0% of the time, Pallas kernels for 0%

profile of v1, /device:TPU:1, one launch (start us, length us, event | category | flops | bytes accessed | tf_op | source)
XLA Modules:
  0.0 969.2 jit_solution(6473975175316476139)
XLA Ops:
  6.5 2.5 fusion.8
  9.0 0.0 copy-start.7
  9.0 1.1 stack.8
  10.1 0.0 copy-done.7
  10.1 5.0 all-to-all-start
  15.1 0.0 all-reduce.5.cloned.1.call-start
  15.2 13.4 %all-to-all-done = f32[4,128,512]{2,1,0:T(8,128)S(1)} async-done(((f32[4,128,512]{2,1,0:T(8,128)}), f32[4,128,512]{2,1,0:T(8,128)S(1)}, u32[]{:S(2)}, u32[]{:S(2)}) %all-to-all-start) | async-done | bytes 1048608 | tf_op jit(solution)/shard_map/all_to_all | solution.py:43
  28.6 1.1 broadcast_select_fusion.3
  29.7 0.0 all-reduce.5.cloned.1.call-update
  29.7 0.0 reduce-scatter.5.cloned.1.call-start
  29.8 0.0 copy-start.1
  29.8 186.6 %all-reduce.5.cloned.1.call-done = f32[512,512]{1,0:T(8,128)} async-done(((f32[512,512]{1,0:T(8,128)}), f32[512,512]{1,0:T(8,128)}) %all-reduce.5.cloned.1.call-update) | async-done | bytes 1048592 | tf_op jit(solution)/shard_map/psum | solution.py:9
  216.3 0.0 copy-done
  216.3 4.1 fusion.10
  220.4 0.0 reduce-scatter.5.cloned.1.call-update
  220.4 22.8 %reduce-scatter.5.cloned.1.call-done = f32[128,512]{1,0:T(8,128)} async-done(((f32[512,512]{1,0:T(8,128)}), f32[128,512]{1,0:T(8,128)}) %reduce-scatter.5.cloned.1.call-update) | async-done | bytes 262160 | tf_op jit(solution)/shard_map/reduce_scatter | solution.py:36
  243.2 0.0 copy-done.1
  243.2 2.5 fusion.6
  245.7 1.1 stack.9
  246.8 3.5 all-to-all-start.1
  250.3 0.0 all-reduce.7.cloned.1.call-start
  250.4 13.0 %all-to-all-done.1 = f32[4,128,512]{2,1,0:T(8,128)S(1)} async-done(((f32[4,128,512]{2,1,0:T(8,128)}), f32[4,128,512]{2,1,0:T(8,128)S(1)}, u32[]{:S(2)}, u32[]{:S(2)}) %all-to-all-start.1) | async-done | bytes 1048608 | tf_op jit(solution)/shard_map/all_to_all | solution.py:43
  263.4 1.1 broadcast_select_fusion.2
  264.5 0.0 all-reduce.7.cloned.1.call-update
  264.5 0.0 reduce-scatter.7.cloned.1.call-start
  264.6 185.5 %all-reduce.7.cloned.1.call-done = f32[512,512]{1,0:T(8,128)} async-done(((f32[512,512]{1,0:T(8,128)}), f32[512,512]{1,0:T(8,128)}) %all-reduce.7.cloned.1.call-update) | async-done | bytes 1048592 | tf_op jit(solution)/shard_map/psum | solution.py:9
  450.0 1.4 select_select_fusion
  451.5 2.8 fusion.14
  454.3 0.0 reduce-scatter.7.cloned.1.call-update
  454.3 22.8 %reduce-scatter.7.cloned.1.call-done = f32[128,512]{1,0:T(8,128)} async-done(((f32[512,512]{1,0:T(8,128)}), f32[128,512]{1,0:T(8,128)}) %reduce-scatter.7.cloned.1.call-update) | async-done | bytes 262160 | tf_op jit(solution)/shard_map/reduce_scatter | solution.py:36
  477.1 2.6 fusion.4
  479.7 0.0 copy-start.3
  479.7 0.7 copy-done.3
  480.4 1.1 stack.10
  481.5 4.2 all-to-all-start.2
  485.8 0.0 all-reduce.9.cloned.1.call-start
  485.8 13.1 %all-to-all-done.2 = f32[4,128,512]{2,1,0:T(8,128)} async-done(((f32[4,128,512]{2,1,0:T(8,128)}), f32[4,128,512]{2,1,0:T(8,128)}, u32[]{:S(2)}, u32[]{:S(2)}) %all-to-all-start.2) | async-done | bytes 1048608 | tf_op jit(solution)/shard_map/all_to_all | solution.py:43
  498.9 1.1 broadcast_select_fusion.1
  500.0 0.0 all-reduce.9.cloned.1.call-update
  500.0 0.0 reduce-scatter.9.cloned.1.call-start
  500.1 186.0 %all-reduce.9.cloned.1.call-done = f32[512,512]{1,0:T(8,128)} async-done(((f32[512,512]{1,0:T(8,128)}), f32[512,512]{1,0:T(8,128)}) %all-reduce.9.cloned.1.call-update) | async-done | bytes 1048592 | tf_op jit(solution)/shard_map/psum | solution.py:9
  686.0 2.8 fusion.12
  688.8 0.0 reduce-scatter.9.cloned.1.call-update
  688.9 25.3 %reduce-scatter.9.cloned.1.call-done = f32[128,512]{1,0:T(8,128)} async-done(((f32[512,512]{1,0:T(8,128)}), f32[128,512]{1,0:T(8,128)}) %reduce-scatter.9.cloned.1.call-update) | async-done | bytes 262160 | tf_op jit(solution)/shard_map/reduce_scatter | solution.py:36
  714.1 2.6 fusion.2
  716.7 0.0 copy-start.5
  716.7 0.7 copy-done.5
  717.4 1.1 stack.11
  718.5 4.2 all-to-all-start.3
  722.8 0.0 all-reduce.11.cloned.1.call-start
  722.8 13.1 %all-to-all-done.3 = f32[4,128,512]{2,1,0:T(8,128)} async-done(((f32[4,128,512]{2,1,0:T(8,128)}), f32[4,128,512]{2,1,0:T(8,128)}, u32[]{:S(2)}, u32[]{:S(2)}) %all-to-all-start.3) | async-done | bytes 1048608 | tf_op jit(solution)/shard_map/all_to_all | solution.py:43
  736.0 1.1 broadcast_select_fusion
  737.1 0.0 all-reduce.11.cloned.1.call-update
  737.1 0.2 reduce-scatter.11.cloned.1.call-start
  737.3 185.1 %all-reduce.11.cloned.1.call-done = f32[512,512]{1,0:T(8,128)} async-done(((f32[512,512]{1,0:T(8,128)}), f32[512,512]{1,0:T(8,128)}) %all-reduce.11.cloned.1.call-update) | async-done | bytes 1048592 | tf_op jit(solution)/shard_map/psum | solution.py:9
  922.4 4.9 fusion
  927.3 0.0 reduce-scatter.11.cloned.1.call-update
  927.4 32.8 %reduce-scatter.11.cloned.1.call-done = f32[128,1024]{1,0:T(8,128)} async-done(((f32[512,1024]{1,0:T(8,128)}), f32[128,1024]{1,0:T(8,128)}) %reduce-scatter.11.cloned.1.call-update) | async-done | bytes 524304 | tf_op jit(solution)/shard_map/reduce_scatter | solution.py:54
  960.2 0.0 copy-done.2
  960.2 1.1 sub.15
  961.3 0.0 copy-done.4
  961.4 0.2 slice_select_fusion
  961.5 0.0 copy-start.9
  961.5 0.8 copy-done.9
  (8 shorter events, 0.0 us)
Async XLA Ops:
  9.0 1.1 copy-start.7
  10.1 18.4 %all-to-all-start = ((f32[4,128,512]{2,1,0:T(8,128)}), f32[4,128,512]{2,1,0:T(8,128)S(1)}, u32[]{:S(2)}, u32[]{:S(2)}) async-start(f32[4,128,512]{2,1,0:T(8,128)} %stack.8), calls=%async_computation | async-start | bytes 2097152 | tf_op jit(solution)/shard_map/all_to_all | solution.py:43
  15.1 201.2 %copy-start = (f32[1024,512]{1,0:T(8,128)S(1)}, f32[1024,512]{1,0:T(8,128)}, u32[]{:S(2)}) copy-start(f32[1024,512]{1,0:T(8,128)} %param.4) | copy-start | bytes 6291460
  15.1 201.2 %all-reduce.5.cloned.1.call-start = ((), (), s32[]{:S(2)}) async-start(), calls=%async_computation.8 | async-start | bytes 2097152 | tf_op jit(solution)/shard_map/psum | solution.py:9
  29.7 213.5 %reduce-scatter.5.cloned.1.call-start = ((), (), s32[]{:S(2)}) async-start(), calls=%async_computation.9 | async-start | bytes 1310720 | tf_op jit(solution)/shard_map/reduce_scatter | solution.py:36
  29.8 213.5 %copy-start.1 = (f32[128,1024]{1,0:T(8,128)S(1)}, f32[128,1024]{1,0:T(8,128)}, u32[]{:S(2)}) copy-start(f32[128,1024]{1,0:T(8,128)} %param.3) | copy-start | bytes 1572868
  246.8 16.6 %all-to-all-start.1 = ((f32[4,128,512]{2,1,0:T(8,128)}), f32[4,128,512]{2,1,0:T(8,128)S(1)}, u32[]{:S(2)}, u32[]{:S(2)}) async-start(f32[4,128,512]{2,1,0:T(8,128)} %stack.9), calls=%async_computation.2 | async-start | bytes 2097152 | tf_op jit(solution)/shard_map/all_to_all | solution.py:43
  250.3 199.7 %all-reduce.7.cloned.1.call-start = ((), (), s32[]{:S(2)}) async-start(), calls=%async_computation.10 | async-start | bytes 2097152 | tf_op jit(solution)/shard_map/psum | solution.py:9
  264.5 212.6 %reduce-scatter.7.cloned.1.call-start = ((), (), s32[]{:S(2)}) async-start(), calls=%async_computation.11 | async-start | bytes 1310720 | tf_op jit(solution)/shard_map/reduce_scatter | solution.py:36
  479.7 0.7 copy-start.3
  481.5 17.4 %all-to-all-start.2 = ((f32[4,128,512]{2,1,0:T(8,128)}), f32[4,128,512]{2,1,0:T(8,128)}, u32[]{:S(2)}, u32[]{:S(2)}) async-start(f32[4,128,512]{2,1,0:T(8,128)} %stack.10), calls=%async_computation.4 | async-start | bytes 2097152 | tf_op jit(solution)/shard_map/all_to_all | solution.py:43
  485.8 200.3 %all-reduce.9.cloned.1.call-start = ((), (), s32[]{:S(2)}) async-start(), calls=%async_computation.12 | async-start | bytes 2097152 | tf_op jit(solution)/shard_map/psum | solution.py:9
  500.0 214.1 %reduce-scatter.9.cloned.1.call-start = ((), (), s32[]{:S(2)}) async-start(), calls=%async_computation.13 | async-start | bytes 1310720 | tf_op jit(solution)/shard_map/reduce_scatter | solution.py:36
  716.7 0.7 copy-start.5
  718.5 17.4 %all-to-all-start.3 = ((f32[4,128,512]{2,1,0:T(8,128)}), f32[4,128,512]{2,1,0:T(8,128)}, u32[]{:S(2)}, u32[]{:S(2)}) async-start(f32[4,128,512]{2,1,0:T(8,128)} %stack.11), calls=%async_computation.6 | async-start | bytes 2097152 | tf_op jit(solution)/shard_map/all_to_all | solution.py:43
  722.8 199.7 %all-reduce.11.cloned.1.call-start = ((), (), s32[]{:S(2)}) async-start(), calls=%async_computation.14 | async-start | bytes 2097152 | tf_op jit(solution)/shard_map/psum | solution.py:9
  737.1 223.1 %reduce-scatter.11.cloned.1.call-start = ((), (), s32[]{:S(2)}) async-start(), calls=%async_computation.15 | async-start | bytes 2621440 | tf_op jit(solution)/shard_map/reduce_scatter | solution.py:54
  927.3 32.9 %copy-start.2 = (f32[128,1024]{1,0:T(8,128)S(1)}, f32[128,1024]{1,0:T(8,128)}, u32[]{:S(2)}) copy-start(f32[128,1024]{1,0:T(8,128)} %param.3) | copy-start | bytes 1572868
  927.3 34.0 %copy-start.4 = (f32[128,512]{1,0:T(8,128)S(1)}, f32[128,512]{1,0:T(8,128)}, u32[]{:S(2)}) copy-start(f32[128,512]{1,0:T(8,128)} %copy-done.3) | copy-start | bytes 786436
  927.3 34.0 %copy-start.6 = (f32[128,512]{1,0:T(8,128)S(1)}, f32[128,512]{1,0:T(8,128)}, u32[]{:S(2)}) copy-start(f32[128,512]{1,0:T(8,128)} %copy-done.5) | copy-start | bytes 786436
  927.3 34.0 %copy-start.8 = (f32[128,512]{1,0:T(8,128)S(1)}, f32[128,512]{1,0:T(8,128)}, u32[]{:S(2)}) copy-start(f32[128,512]{1,0:T(8,128)} %copy-done.7) | copy-start | bytes 786436
  961.5 0.8 copy-start.9
Sparse Core Ops, SparseCore 0:
  29.8 186.4 all-reduce.4
  220.5 22.6 reduce-scatter.4
  264.6 185.3 all-reduce.6
  454.5 22.6 reduce-scatter.6
  500.1 185.8 all-reduce.8
  689.0 25.1 reduce-scatter.8
  737.2 185.1 all-reduce.10
  927.5 32.6 reduce-scatter.10
